TPU v7x, 256 devices: a whole 4x4x8 slice. The times are simulated.
256 devices in a mesh: node: 8 (over z_lo, core), drow: 4 (over x), dcol: 8 (over z_hi, y).
Axes of the slice: x: 4, y: 4, z: 8 (z_hi: 2, z_lo: 4; z = z_hi * 4 + z_lo), core: 2. Of those that a mesh axis runs over, the one named last changes fastest.
Arguments:
- freq_resp: bfloat16 [2, 8, 4096, 8192], P(None, None, ('drow', 'dcol'), 'node'), may hold values from -0.0625 to 0.0625
- node_coords: int32 [2, 8192], P(None, 'node'), may hold values from 0 to 1023
- heading_steps: int32 [2, 512], replicated, may hold values from -8 to 8
- spectral_weights: int32 [8, 512], replicated, may hold values from 1 to 64
Outputs:
- cross_spectra: float32 [2, 8, 4, 1024, 4096], P(None, None, 'drow', 'node', 'dcol')
All inputs are finite; a program needn't handle non-finite values.
Results may differ from a plain program's by a relative error of at most 0.0038.
Values may be sent and summed in bfloat16 or wider, within the bound.
No kernel may reach another device: no remote copies, remote signals or barrier semaphores. Data moves between devices by JAX's collectives and lax.ppermute only.
A program may use at most 128 MiB of HBM per device.

v0:
```python
import math
import jax
import jax.numpy as jnp
from jax import lax
from jax.sharding import PartitionSpec as P

DIRS = 512
FREQS = 8
GRID = 1024


def unit_phasor(turn):
    quarter = GRID // 4
    shifted = turn + quarter // 2 & GRID - 1
    quadrant = shifted >> 8
    offset = (shifted & quarter - 1) - quarter // 2
    x = offset.astype(jnp.float32) * (2.0 * math.pi / GRID)
    x2 = x * x
    s = x * (1.0 + x2 * (-1.0 / 6 + x2 * (1.0 / 120 + x2 * (-1.0 / 5040 + x2 * (1.0 / 362880)))))
    c = 1.0 + x2 * (-0.5 + x2 * (1.0 / 24 + x2 * (-1.0 / 720 + x2 * (1.0 / 40320))))
    odd = quadrant & 1 == 1
    cos_mag = jnp.where(odd, s, c)
    sin_mag = jnp.where(odd, c, s)
    cos_neg = (quadrant == 1) | (quadrant == 2)
    sin_neg = quadrant >= 2
    return (jnp.where(cos_neg, -cos_mag, cos_mag), jnp.where(sin_neg, -sin_mag, sin_mag))


def excitation(coords, heading_steps, spectral_weights):
    freq_index = (jnp.arange(FREQS, dtype=jnp.int32) + 1)[:, None, None]
    project = (
        coords[0][:, None] * heading_steps[0][None, :]
        + coords[1][:, None] * heading_steps[1][None, :]
    )
    turn_count = freq_index * project[None] & GRID - 1
    cos_t, sin_t = unit_phasor(turn_count)
    spread = jnp.sqrt(spectral_weights.astype(jnp.float32) / (64.0 * DIRS))[:, None, :]
    load_re = (spread * cos_t).astype(jnp.bfloat16)
    load_im = (-spread * sin_t).astype(jnp.bfloat16)
    return (load_re, load_im)


def local(freq_resp, node_coords, heading_steps, spectral_weights):
    load_re, load_im = excitation(node_coords, heading_steps, spectral_weights)
    right = jnp.stack(
        [
            jnp.concatenate([load_re, load_im], axis=-1),
            jnp.concatenate([-load_im, load_re], axis=-1),
        ],
        axis=0,
    )
    partial_amp = jnp.einsum("pfkn,pfne->fke", freq_resp, right, preferred_element_type=jnp.float32)
    amplitudes = lax.psum_scatter(partial_amp, "node", scatter_dimension=1, tiled=True).astype(
        jnp.bfloat16
    )
    cols = lax.all_gather(amplitudes, ("node", "drow"), axis=1, tiled=True)
    rows = lax.all_gather(amplitudes, "dcol", axis=1, tiled=True)
    rows_im = jnp.concatenate([rows[..., DIRS:], -rows[..., :DIRS]], axis=-1)
    lead = jnp.stack([rows, rows_im], axis=0)
    spec = jnp.einsum("pfke,fje->pfkj", lead, cols, preferred_element_type=jnp.float32)
    return spec[:, :, None]


def solution(mesh):
    placed = (P(None, None, ("drow", "dcol"), "node"), P(None, "node"), P(), P())
    return jax.shard_map(
        local,
        mesh=mesh,
        in_specs=placed,
        out_specs=P(None, None, "drow", "node", "dcol"),
        check_vma=False,
    )
```

profile of v0, /device:TPU:1, one launch (start us, length us, event | category | flops | bytes accessed | tf_op | source)
XLA Modules:
  0.0 358.4 jit_solution(1211883478855104320)
XLA Ops:
  6.5 0.0 reduce-scatter.2.cloned.1.call-start
  6.5 0.8 fusion.37
  7.3 0.8 fusion.36
  8.1 0.7 fusion.33
  8.8 0.4 multiply_add_fusion.1
  9.2 22.0 %fusion.34 = bf16[8,1024,512]{1,2,0:T(8,128)(2,1)} fusion(s32[1024,512]{0,1:T(8,128)S(1)} %multiply_add_fusion.1, s32[8]{0:T(128)S(1)} %iota_add_fusion, f32[8,512]{1,0:T(8,128)S(1)} %get-tuple-element.13), kind=kLoop, calls=%fused_computation.43 | loop fusion | flops 159383552 | bytes 10502176 | tf_op jit(solution)/shard_map/neg | solution.py:48
  31.2 26.0 %fusion.7 = (bf16[8,1024,512]{1,2,0:T(8,128)(2,1)}, bf16[8,1024,512]{1,2,0:T(8,128)(2,1)}) fusion(f32[8,512]{1,0:T(8,128)S(1)} %get-tuple-element.13, s32[1024,512]{0,1:T(8,128)S(1)} %multiply_add_fusion.1, s32[8]{0:T(128)S(1)} %iota_add_fusion, f32[8,512]{1,0:T(8,128)S(1)} %get-tuple-element.14), kind=kLoop, calls=%fused_computation.9 | loop fusion | flops 180355072 | bytes 18907168 | tf_op jit(solution)/shard_map/convert_element_type | solution.py:39
  57.2 24.9 %maximum_bitcast_fusion = (bf16[1,8,1024,1024]{2,3,0,1:T(8,128)(2,1)}, bf16[1,8,1024,1024]{2,3,0,1:T(8,128)(2,1)}) fusion(bf16[8,1024,512]{1,2,0:T(8,128)(2,1)} %get-tuple-element.7, bf16[8,1024,512]{1,2,0:T(8,128)(2,1)} %get-tuple-element.8, bf16[8,1024,512]{1,2,0:T(8,128)(2,1)} %fusion.34), kind=kLoop, calls=%fused_computation.10 | loop fusion | flops 67108864 | bytes 58720256 | tf_op jit(solution)/shard_map/stack | solution.py:45
  82.1 17.9 %fusion.26 = f32[8,128,1024]{1,2,0:T(8,128)} fusion(bf16[2,8,128,1024]{3,2,1,0:T(8,128)(2,1)} %param.4, bf16[1,8,1024,1024]{2,3,0,1:T(8,128)(2,1)} %get-tuple-element.6, bf16[1,8,1024,1024]{2,3,0,1:T(8,128)(2,1)} %get-tuple-element.5), kind=kOutput, calls=%fused_computation.33 | convolution fusion | flops 4311744512 | bytes 41943040 | tf_op jit(solution)/shard_map/pfkn,pfne->fke/dot_general | solution.py:52
  100.0 5.5 %copy.12 = f32[8,128,1024]{2,0,1:T(8,128)} copy(f32[8,128,1024]{1,2,0:T(8,128)} %fusion.26) | data formatting | bytes 8388608 | tf_op jit(solution)/shard_map/pfkn,pfne->fke/dot_general | solution.py:52
  105.5 0.0 reduce-scatter.2.cloned.1.call-update
  105.5 0.0 all-gather.5.cloned.1.call-start
  105.6 56.8 %reduce-scatter.2.cloned.1.call-done = f32[8,16,1024]{2,0,1:T(8,128)} async-done(((f32[8,128,1024]{2,0,1:T(8,128)}), f32[8,16,1024]{2,0,1:T(8,128)}) %reduce-scatter.2.cloned.1.call-update) | async-done | bytes 524304 | tf_op jit(solution)/shard_map/reduce_scatter | solution.py:53
  162.4 1.8 convert_element_type.19
  164.2 0.0 all-gather.5.cloned.1.call-update
  164.2 0.2 all-gather.3.cloned.1.call-start
  164.4 0.5 all-gather.3.cloned.1.call-update
  164.9 76.3 %all-gather.5.cloned.1.call-done = bf16[8,128,1024]{2,0,1:T(8,128)(2,1)} async-done(((bf16[8,16,1024]{2,0,1:T(8,128)(2,1)}), bf16[8,128,1024]{2,0,1:T(8,128)(2,1)}) %all-gather.5.cloned.1.call-update) | async-done | bytes 2097168 | tf_op jit(solution)/shard_map/all_gather | solution.py:57
  241.2 2.7 copy.32
  243.9 0.1 fusion.35
  244.1 1.6 maximum_bitcast_fusion.2
  245.6 89.8 %all-gather.3.cloned.1.call-done = bf16[8,512,1024]{2,0,1:T(8,128)(2,1)} async-done(((bf16[8,16,1024]{2,0,1:T(8,128)(2,1)}), bf16[8,512,1024]{2,0,1:T(8,128)(2,1)}) %all-gather.3.cloned.1.call-update) | async-done | bytes 8388624 | tf_op jit(solution)/shard_map/all_gather | solution.py:56
  335.5 11.0 %fusion.21 = f32[2,8,1,128,512]{3,4,0,1,2:T(8,128)} fusion(bf16[1,8,128,1024]{3,2,0,1:T(8,128)(2,1)} %maximum_bitcast_fusion.2, bf16[1,8,128,1024]{3,2,0,1:T(8,128)(2,1)S(1)} %bitcast.25, bf16[8,512,1024,1]{2,0,1,3:T(8,128)(2,1)} %bitcast.30), kind=kOutput, calls=%fused_computation.32 | convolution fusion | flops 2155872256 | bytes 16777216 | tf_op jit(solution)/shard_map/pfke,fje->pfkj/dot_general | solution.py:60
  346.5 5.3 %copy.17 = f32[2,8,1,128,512]{4,3,2,1,0:T(8,128)} copy(f32[2,8,1,128,512]{3,4,0,1,2:T(8,128)} %fusion.21) | data formatting | bytes 8388608 | tf_op jit(solution)/shard_map/broadcast_in_dim | solution.py:61
  (1 shorter events, 0.0 us)
Async XLA Ops:
  6.5 155.8 %reduce-scatter.2.cloned.1.call-start = ((), (), s32[]{:S(2)}) async-start(), calls=%async_computation.1 | async-start | bytes 4718592 | tf_op jit(solution)/shard_map/reduce_scatter | solution.py:53
  105.5 135.6 %all-gather.5.cloned.1.call-start = ((), (), s32[]{:S(2)}) async-start(), calls=%async_computation.3 | async-start | bytes 2359296 | tf_op jit(solution)/shard_map/all_gather | solution.py:57
  164.2 171.3 %all-gather.3.cloned.1.call-start = ((), (), s32[]{:S(2)}) async-start(), calls=%async_computation.2 | async-start | bytes 8650752 | tf_op jit(solution)/shard_map/all_gather | solution.py:56
Sparse Core Ops, SparseCore 0:
  105.7 56.6 reduce-scatter.1
  165.0 76.1 all-gather.4
  243.0 92.4 all-gather.2
where the time goes:
time: 359 us; the launch traced here: 358 us
  waiting for transfers between devices  223 us (62%)
  other arithmetic  77.5 us (22%)
  matrix products  28.9 us (8%)
  local copies, waits for them, and re-layouts  15.1 us (4%)
  between operations  13.1 us (4%)
    all_gather x1, waiting for transfers between devices, local(): cols = lax.all_gather(amplitudes, ('node', 'drow'), axis=1, tiled=True)  89.8 us
    all_gather x1, waiting for transfers between devices, local(): rows = lax.all_gather(amplitudes, 'dcol', axis=1, tiled=True)  76.3 us
    reduce_scatter x1, waiting for transfers between devices, local(): lax.psum_scatter(partial_amp, 'node', scatter_dimension=1, tiled=True)  56.8 us
    convert_element_type x1, other arithmetic, excitation(): load_im = (-spread * sin_t).astype(jnp.bfloat16)  26 us
    another operation x1, other arithmetic, local(): jnp.stack([jnp.concatenate([load_re, load_im], axis=-1), jnp.concatenate(...  24.9 us
    neg x1, other arithmetic, local(): -load_im  22 us
    dot_general x1, matrix products, local(): jnp.einsum('pfkn,pfne->fke', freq_resp, right, preferred_element_type=jnp...  17.9 us
    dot_general x1, matrix products, local(): jnp.einsum('pfke,fje->pfkj', lead, cols, preferred_element_type=jnp.float32)  11 us
  transfers between devices with their start and end apart: 3, of which 3 were waited for; matrix products, arithmetic and copies ran while one was open for 1% of the time, Pallas kernels for 0%

commit v1 on v0

--- a/solution.py
+++ b/solution.py
@@ -7,6 +7,11 @@
 DIRS = 512
 FREQS = 8
 GRID = 1024
+
+
+def gather_over(shard, name, dim):
+    stack = jnp.stack([shard] * lax.axis_size(name))
+    return jnp.concatenate(lax.all_to_all(stack, name, 0, 0), axis=dim)
 
 
 def unit_phasor(turn):
@@ -53,7 +58,7 @@
     amplitudes = lax.psum_scatter(partial_amp, "node", scatter_dimension=1, tiled=True).astype(
         jnp.bfloat16
     )
-    cols = lax.all_gather(amplitudes, ("node", "drow"), axis=1, tiled=True)
+    cols = gather_over(amplitudes, ("node", "drow"), 1)
     rows = lax.all_gather(amplitudes, "dcol", axis=1, tiled=True)
     rows_im = jnp.concatenate([rows[..., DIRS:], -rows[..., :DIRS]], axis=-1)
     lead = jnp.stack([rows, rows_im], axis=0)

time: 359 us -> 422 us (1.18)
  waiting for transfers between devices: 223 us -> 268 us
  local copies, waits for them, and re-layouts: 15.1 us -> 28.2 us
  starting transfers between devices: 0.27 us -> 7.89 us
    all_to_all x0 -> x1, waiting for transfers between devices: none -> 119 us  [gather_over(): return jnp.concatenate(lax.all_to_all(stack, name, 0, 0), axis=dim)]
    all_gather x1 -> x0, waiting for transfers between devices: 89.8 us -> none  [local(): cols = lax.all_gather(amplitudes, ('node', 'drow'), axis=1, tiled=True)]
    all_gather x1, waiting for transfers between devices: 76.3 us -> 91.7 us  [local(): rows = lax.all_gather(amplitudes, 'dcol', axis=1, tiled=True)]
    reshape x0 -> x1, local copies, waits for them, and re-layouts: none -> 8.68 us  [gather_over(): return jnp.concatenate(lax.all_to_all(stack, name, 0, 0), axis=dim)]
    all_to_all x0 -> x1, starting transfers between devices: none -> 7.66 us  [gather_over(): return jnp.concatenate(lax.all_to_all(stack, name, 0, 0), axis=dim)]
    another operation x0 -> x1, local copies, waits for them, and re-layouts: none -> 4.3 us  [gather_over(): stack = jnp.stack([shard] * lax.axis_size(name))]
where the time goes in v1:
time: 422 us
  waiting for transfers between devices  268 us (64%)
  other arithmetic  76.7 us (18%)
  local copies, waits for them, and re-layouts  28.2 us (7%)
  matrix products  27.5 us (7%)
  between operations  13.5 us (3%)
  starting transfers between devices  7.89 us (2%)
    all_to_all x1, waiting for transfers between devices, gather_over(): return jnp.concatenate(lax.all_to_all(stack, name, 0, 0), axis=dim)  119 us
    all_gather x1, waiting for transfers between devices, local(): rows = lax.all_gather(amplitudes, 'dcol', axis=1, tiled=True)  91.7 us
    reduce_scatter x1, waiting for transfers between devices, local(): lax.psum_scatter(partial_amp, 'node', scatter_dimension=1, tiled=True)  56.8 us
    convert_element_type x1, other arithmetic, excitation(): load_im = (-spread * sin_t).astype(jnp.bfloat16)  25.9 us
    another operation x1, other arithmetic, local(): jnp.stack([jnp.concatenate([load_re, load_im], axis=-1), jnp.concatenate(...  24.8 us
    neg x1, other arithmetic, local(): -load_im  22 us
    dot_general x1, matrix products, local(): jnp.einsum('pfkn,pfne->fke', freq_resp, right, preferred_element_type=jnp...  17.9 us
    dot_general x1, matrix products, local(): jnp.einsum('pfke,fje->pfkj', lead, cols, preferred_element_type=jnp.float32)  9.57 us
  transfers between devices with their start and end apart: 3, of which 3 were waited for; matrix products, arithmetic and copies ran while one was open for 1% of the time, Pallas kernels for 0%

profile of v1, /device:TPU:1, one launch (start us, length us, event | category | flops | bytes accessed | tf_op | source)
XLA Modules:
  0.0 421.5 jit_solution(7686834050441413872)
XLA Ops:
  6.5 0.0 reduce-scatter.2.cloned.1.call-start
  6.5 0.8 fusion.34
  7.3 0.8 fusion.33
  8.1 0.7 fusion.30
  8.8 0.4 multiply_add_fusion.1
  9.2 22.0 %fusion.31 = bf16[8,1024,512]{1,2,0:T(8,128)(2,1)} fusion(s32[1024,512]{0,1:T(8,128)S(1)} %multiply_add_fusion.1, s32[8]{0:T(128)S(1)} %iota_add_fusion, f32[8,512]{1,0:T(8,128)S(1)} %get-tuple-element.13), kind=kLoop, calls=%fused_computation.42 | loop fusion | flops 159383552 | bytes 10502176 | tf_op jit(solution)/shard_map/neg | solution.py:53
  31.2 25.9 %fusion.7 = (bf16[8,1024,512]{1,2,0:T(8,128)(2,1)}, bf16[8,1024,512]{1,2,0:T(8,128)(2,1)}) fusion(f32[8,512]{1,0:T(8,128)S(1)} %get-tuple-element.13, s32[1024,512]{0,1:T(8,128)S(1)} %multiply_add_fusion.1, s32[8]{0:T(128)S(1)} %iota_add_fusion, f32[8,512]{1,0:T(8,128)S(1)} %get-tuple-element.14), kind=kLoop, calls=%fused_computation.9 | loop fusion | flops 180355072 | bytes 18907168 | tf_op jit(solution)/shard_map/convert_element_type | solution.py:44
  57.2 24.8 %maximum_bitcast_fusion = (bf16[1,8,1024,1024]{2,3,0,1:T(8,128)(2,1)}, bf16[1,8,1024,1024]{2,3,0,1:T(8,128)(2,1)}) fusion(bf16[8,1024,512]{1,2,0:T(8,128)(2,1)} %get-tuple-element.7, bf16[8,1024,512]{1,2,0:T(8,128)(2,1)} %get-tuple-element.8, bf16[8,1024,512]{1,2,0:T(8,128)(2,1)} %fusion.31), kind=kLoop, calls=%fused_computation.10 | loop fusion | flops 67108864 | bytes 58720256 | tf_op jit(solution)/shard_map/stack | solution.py:50
  82.0 17.9 %fusion.23 = f32[8,128,1024]{1,2,0:T(8,128)} fusion(bf16[2,8,128,1024]{3,2,1,0:T(8,128)(2,1)} %param.4, bf16[1,8,1024,1024]{2,3,0,1:T(8,128)(2,1)} %get-tuple-element.6, bf16[1,8,1024,1024]{2,3,0,1:T(8,128)(2,1)} %get-tuple-element.5), kind=kOutput, calls=%fused_computation.32 | convolution fusion | flops 4311744512 | bytes 41943040 | tf_op jit(solution)/shard_map/pfkn,pfne->fke/dot_general | solution.py:57
  99.9 5.5 %copy.12 = f32[8,128,1024]{2,0,1:T(8,128)} copy(f32[8,128,1024]{1,2,0:T(8,128)} %fusion.23) | data formatting | bytes 8388608 | tf_op jit(solution)/shard_map/pfkn,pfne->fke/dot_general | solution.py:57
  105.4 0.0 reduce-scatter.2.cloned.1.call-update
  105.4 56.8 %reduce-scatter.2.cloned.1.call-done = f32[8,16,1024]{2,0,1:T(8,128)} async-done(((f32[8,128,1024]{2,0,1:T(8,128)}), f32[8,16,1024]{2,0,1:T(8,128)}) %reduce-scatter.2.cloned.1.call-update) | async-done | bytes 524304 | tf_op jit(solution)/shard_map/reduce_scatter | solution.py:58
  162.3 1.1 convert_element_type.19
  163.3 0.0 copy-start
  163.3 0.2 copy.13
  163.5 4.3 %stack.17 = bf16[32,8,16,1024]{3,2,1,0:T(8,128)(2,1)} broadcast(bf16[8,16,1024]{2,1,0:T(8,128)(2,1)S(1)} %copy.13), dimensions={1,2,3} | broadcast | bytes 8650752 | tf_op jit(solution)/shard_map/stack | solution.py:13
  167.8 7.7 %all-to-all-start = ((bf16[32,8,16,1024]{3,2,1,0:T(8,128)(2,1)}), bf16[32,8,16,1024]{3,2,1,0:T(8,128)(2,1)}, u32[]{:S(2)}, u32[]{:S(2)}) async-start(bf16[32,8,16,1024]{3,2,1,0:T(8,128)(2,1)} %stack.17), calls=%async_computation.1 | async-start | bytes 16777216 | tf_op jit(solution)/shard_map/all_to_all | solution.py:14
  175.5 0.2 all-gather.2.cloned.1.call-start
  175.7 0.0 copy-done
  175.7 0.5 all-gather.2.cloned.1.call-update
  176.2 91.7 %all-gather.2.cloned.1.call-done = bf16[8,128,1024]{2,0,1:T(8,128)(2,1)} async-done(((bf16[8,16,1024]{2,0,1:T(8,128)(2,1)}), bf16[8,128,1024]{2,0,1:T(8,128)(2,1)}) %all-gather.2.cloned.1.call-update) | async-done | bytes 2097168 | tf_op jit(solution)/shard_map/all_gather | solution.py:62
  267.9 2.7 copy.27
  270.6 0.1 fusion.32
  270.8 1.6 maximum_bitcast_fusion.2
  272.4 118.7 %all-to-all-done = bf16[32,8,16,1024]{3,2,1,0:T(8,128)(2,1)} async-done(((bf16[32,8,16,1024]{3,2,1,0:T(8,128)(2,1)}), bf16[32,8,16,1024]{3,2,1,0:T(8,128)(2,1)}, u32[]{:S(2)}, u32[]{:S(2)}) %all-to-all-start) | async-done | bytes 8388640 | tf_op jit(solution)/shard_map/all_to_all | solution.py:14
  391.1 0.0 copy-start.1
  391.1 8.7 %copy.14 = bf16[8,32,16,1024]{3,2,1,0:T(8,128)(2,1)} copy(bf16[8,32,16,1024]{3,2,0,1:T(8,128)(2,1)} %bitcast.10) | data formatting | bytes 16777216 | tf_op jit(solution)/shard_map/reshape | solution.py:14
  399.8 0.0 copy-done.1
  399.8 9.6 %fusion.20 = f32[2,8,1,128,512]{3,4,0,1,2:T(8,128)} fusion(bf16[8,512,1024,1]{2,1,3,0:T(8,128)(2,1)} %bitcast.31, bf16[1,8,128,1024]{3,2,0,1:T(8,128)(2,1)S(1)} %copy-done.1, bf16[1,8,128,1024]{3,2,0,1:T(8,128)(2,1)S(1)} %bitcast.32), kind=kOutput, calls=%fused_computation.31 | convolution fusion | flops 2155872256 | bytes 16777216 | tf_op jit(solution)/shard_map/pfke,fje->pfkj/dot_general | solution.py:65
  409.3 5.3 %copy.18 = f32[2,8,1,128,512]{4,3,2,1,0:T(8,128)} copy(f32[2,8,1,128,512]{3,4,0,1,2:T(8,128)} %fusion.20) | data formatting | bytes 8388608 | tf_op jit(solution)/shard_map/broadcast_in_dim | solution.py:66
  (1 shorter events, 0.0 us)
Async XLA Ops:
  6.5 155.7 %reduce-scatter.2.cloned.1.call-start = ((), (), s32[]{:S(2)}) async-start(), calls=%async_computation.2 | async-start | bytes 4718592 | tf_op jit(solution)/shard_map/reduce_scatter | solution.py:58
  163.3 12.4 %copy-start = (bf16[8,16,1024]{2,0,1:T(8,128)(2,1)}, bf16[8,16,1024]{2,0,1:T(8,128)(2,1)S(1)}, u32[]{:S(2)}) copy-start(bf16[8,16,1024]{2,0,1:T(8,128)(2,1)S(1)} %convert_element_type.19) | copy-start | bytes 786436
  167.8 223.3 %all-to-all-start = ((bf16[32,8,16,1024]{3,2,1,0:T(8,128)(2,1)}), bf16[32,8,16,1024]{3,2,1,0:T(8,128)(2,1)}, u32[]{:S(2)}, u32[]{:S(2)}) async-start(bf16[32,8,16,1024]{3,2,1,0:T(8,128)(2,1)} %stack.17), calls=%async_computation.1 | async-start | bytes 16777216 | tf_op jit(solution)/shard_map/all_to_all | solution.py:14
  175.5 92.4 %all-gather.2.cloned.1.call-start = ((), (), s32[]{:S(2)}) async-start(), calls=%async_computation.3 | async-start | bytes 2359296 | tf_op jit(solution)/shard_map/all_gather | solution.py:62
  391.1 8.7 %copy-start.1 = (bf16[1,8,128,1024]{3,2,0,1:T(8,128)(2,1)S(1)}, bf16[1,8,128,1024]{3,2,0,1:T(8,128)(2,1)}, u32[]{:S(2)}) copy-start(bf16[1,8,128,1024]{3,2,0,1:T(8,128)(2,1)} %maximum_bitcast_fusion.2) | copy-start | bytes 6291460
Sparse Core Ops, SparseCore 0:
  105.5 56.6 reduce-scatter.1
  178.9 88.9 all-gather.1
